TPU v7x, 32 devices: a whole 2x2x4 slice. The times are simulated.
32 devices in a mesh: row: 4 (over z), col: 4 (over y, core), pix: 2 (over x).
Axes of the slice: x: 2, y: 2, z: 4, core: 2. Of those that a mesh axis runs over, the one named last changes fastest.
Arguments:
- sample_frames: bfloat16 [4096, 16384], P(('row', 'col'), 'pix'), may hold values from 0.14 to 26
- reference_frames: bfloat16 [4096, 16384], P(('row', 'col'), 'pix'), may hold values from 0.14 to 26
- gain: float32 [16384], P('pix'), may hold values from 0.5 to 2
- flat: float32 [16384], P('pix'), may hold values from 0.6 to 1.6
- qbin: int32 [16384], P('pix'), may hold values from 0 to 31
- region: int32 [16384], P('pix'), may hold values 0 or 1
- live: int32 [16384], P('pix'), may hold values 0 or 1
Outputs:
- twotime: float32 [4096, 4, 4, 256], P('row', None, 'col', 'pix')
All inputs are finite; a program needn't handle non-finite values. No bound on the sum of `region` or of `live` on one device may be relied on, other than what follows from the above.
Results may differ from a plain program's by a relative error of at most 0.0039.
Values may be sent and summed in bfloat16 or wider, within the bound.
No kernel may reach another device: no remote copies, remote signals or barrier semaphores. Data moves between devices by JAX's collectives and lax.ppermute only.
A program may use at most 128 MiB of HBM per device.

v0:
```python
import math
import jax
import jax.numpy as jnp
from jax import lax
from jax.sharding import PartitionSpec as P

QBINS = 32


def on_device(sample_frames, reference_frames, gain, flat, qbin, region, live):
    block = sample_frames.shape[0]
    factor = gain / flat
    select = (qbin[None, :] == jnp.arange(QBINS, dtype=jnp.int32)[:, None]).astype(jnp.float32)
    ref_select = select * (live * (1 - region)).astype(jnp.float32)[None, :]
    sample_weight = (live * region).astype(jnp.float32)
    corrected_sample = sample_frames.astype(jnp.float32) * factor
    corrected_reference = reference_frames.astype(jnp.float32) * factor
    sums_sample = jnp.dot(corrected_sample, ref_select.T, precision=lax.Precision.HIGHEST)
    sums_reference = jnp.dot(corrected_reference, ref_select.T, precision=lax.Precision.HIGHEST)
    counts = jnp.sum(ref_select, axis=1)
    sums_sample, sums_reference, counts = lax.psum((sums_sample, sums_reference, counts), "pix")
    mean_sample = (sums_sample + 1.0) / (counts + 1.0)
    mean_reference = (sums_reference + 1.0) / (counts + 1.0)
    spread_sample = jnp.dot(mean_sample, select, precision=lax.Precision.HIGHEST)
    spread_reference = jnp.dot(mean_reference, select, precision=lax.Precision.HIGHEST)
    delta_sample = ((corrected_sample / spread_sample - 1.0) * sample_weight).astype(jnp.bfloat16)
    delta_reference = (corrected_reference / spread_reference - 1.0).astype(jnp.bfloat16)
    sample_rows = lax.all_gather(delta_sample, "col", axis=0, tiled=True)
    partial_value = lax.dot_general(
        sample_rows,
        lax.all_gather(delta_reference, "row", axis=0, tiled=True),
        (((1,), (1,)), ((), ())),
        preferred_element_type=jnp.float32,
    )
    groups = lax.axis_size("row")
    scale = 1.0 / math.sqrt(gain.shape[0] * lax.axis_size("pix"))
    partial_value = (partial_value * scale).reshape(sample_rows.shape[0], groups, block)
    whole = lax.psum(partial_value, "pix")
    width = block // lax.axis_size("pix")
    mine = lax.dynamic_slice_in_dim(whole, lax.axis_index("pix") * width, width, 2)
    return mine[:, :, None, :]


def solution(mesh):
    return jax.shard_map(
        on_device,
        mesh=mesh,
        in_specs=(
            P(("row", "col"), "pix"),
            P(("row", "col"), "pix"),
            P("pix"),
            P("pix"),
            P("pix"),
            P("pix"),
            P("pix"),
        ),
        out_specs=P("row", None, "col", "pix"),
        check_vma=False,
    )
```

profile of v0, /device:TPU:0, one launch (start us, length us, event | category | flops | bytes accessed | tf_op | source)
XLA Modules:
  0.0 598.4 jit_solution(18286605986021742596)
XLA Ops:
  6.5 0.0 all-reduce.6.cloned.1.call-start
  6.5 0.8 multiply_convert_fusion.1
  7.3 0.8 div.23
  8.1 1.5 select_reduce_fusion
  9.6 9.2 %fusion.5 = f32[256,32]{1,0:T(8,128)} fusion(bf16[256,8192]{1,0:T(8,128)(2,1)} %param.8, f32[8192]{0:T(1024)S(1)} %div.23, f32[8192]{0:T(1024)S(1)} %get-tuple-element.8, s32[8192]{0:T(1024)} %param.11), kind=kOutput, calls=%fused_computation.8 | convolution fusion | flops 810024960 | bytes 4325376 | tf_op jit(solution)/shard_map/dot_general | solution.py:19
  18.8 9.2 %fusion.6 = f32[256,32]{1,0:T(8,128)} fusion(bf16[256,8192]{1,0:T(8,128)(2,1)} %param.7, f32[8192]{0:T(1024)S(1)} %div.23, f32[8192]{0:T(1024)S(1)} %get-tuple-element.8, s32[8192]{0:T(1024)} %param.11), kind=kOutput, calls=%fused_computation.10 | convolution fusion | flops 810024960 | bytes 4325376 | tf_op jit(solution)/shard_map/dot_general | solution.py:18
  28.0 0.0 all-reduce.6.cloned.1.call-update
  28.1 0.0 all-gather.3.cloned.1.call-start
  28.1 26.4 %all-reduce.6.cloned.1.call-done = (f32[256,32]{1,0:T(8,128)}, f32[32]{0:T(128)}, f32[256,32]{1,0:T(8,128)}) async-done(((f32[256,32]{1,0:T(8,128)}, f32[32]{0:T(128)}, f32[256,32]{1,0:T(8,128)}), (f32[256,32]{1,0:T(8,128)}, f32[32]{0:T(128)}, f32[256,32]{1,0:T(8,128)})) %all-reduce.6.cloned.1.call-update) | async-done | bytes 65680 | tf_op jit(solution)/shard_map/psum | solution.py:21
  54.5 0.6 broadcast_add_fusion
  55.1 0.0 copy-done
  55.1 7.9 %fusion.4 = bf16[256,8192]{1,0:T(8,128)(2,1)} fusion(bf16[256,8192]{1,0:T(8,128)(2,1)} %param.7, f32[8192]{0:T(1024)S(1)} %get-tuple-element.9, f32[8192]{0:T(1024)S(1)} %div.23, s32[8192]{0:T(1024)S(1)} %copy-done, f32[256,32]{1,0:T(8,128)} %get-tuple-element.5, f32[32]{0:T(128)S(1)} %broadcast_add_fusion), kind=kOutput, calls=%fused_computation.6 | convolution fusion | flops 818167808 | bytes 8519808 | tf_op jit(solution)/shard_map/dot_general | solution.py:24
  63.0 0.0 all-gather.3.cloned.1.call-update
  63.0 0.2 all-gather.5.cloned.1.call-start
  63.3 7.6 %fusion.1 = bf16[256,8192]{1,0:T(8,128)(2,1)} fusion(bf16[256,8192]{1,0:T(8,128)(2,1)} %param.8, f32[8192]{0:T(1024)S(1)} %div.23, s32[8192]{0:T(1024)S(1)} %copy-done, f32[256,32]{1,0:T(8,128)S(1)} %copy-done.1, f32[32]{0:T(128)S(1)} %broadcast_add_fusion), kind=kOutput, calls=%fused_computation.2 | convolution fusion | flops 816070656 | bytes 8487040 | tf_op jit(solution)/shard_map/dot_general | solution.py:25
  70.9 0.0 all-gather.5.cloned.1.call-update
  70.9 0.0 all-reduce.4.cloned.1.call-start
  70.9 98.4 %all-gather.3.cloned.1.call-done = bf16[1024,8192]{1,0:T(8,128)(2,1)} async-done(((bf16[256,8192]{1,0:T(8,128)(2,1)}), bf16[1024,8192]{1,0:T(8,128)(2,1)}) %all-gather.3.cloned.1.call-update) | async-done | bytes 16777232 | tf_op jit(solution)/shard_map/all_gather | solution.py:28
  169.3 288.5 %all-gather.5.cloned.1.call-done = bf16[1024,8192]{1,0:T(8,128)(2,1)} async-done(((bf16[256,8192]{1,0:T(8,128)(2,1)}), bf16[1024,8192]{1,0:T(8,128)(2,1)}) %all-gather.5.cloned.1.call-update) | async-done | bytes 16777232 | tf_op jit(solution)/shard_map/all_gather | solution.py:31
  457.8 24.3 %convolution_multiply_fusion = f32[1024,1024]{0,1:T(8,128)} fusion(bf16[1024,8192]{1,0:T(8,128)(2,1)} %all-gather.3.cloned.1.call-done, bf16[1024,8192]{1,0:T(8,128)(2,1)} %all-gather.5.cloned.1.call-done), kind=kOutput, calls=%fused_computation.13 | convolution fusion | flops 17180917760 | bytes 37748736 | tf_op jit(solution)/shard_map/dot_general | solution.py:29
  482.1 0.0 all-reduce.4.cloned.1.call-update
  482.1 106.2 %all-reduce.4.cloned.1.call-done = f32[1024,4,256]{0,2,1:T(8,128)} async-done(((f32[1024,4,256]{0,2,1:T(8,128)}), f32[1024,4,256]{0,2,1:T(8,128)}) %all-reduce.4.cloned.1.call-update) | async-done | bytes 4194320 | tf_op jit(solution)/shard_map/psum | solution.py:38
  588.3 1.7 constant_dynamic-slice_fusion
  590.1 1.8 copy.9
  (3 shorter events, 0.0 us)
Async XLA Ops:
  6.5 48.6 %copy-start = (s32[8192]{0:T(1024)S(1)}, s32[8192]{0:T(1024)}, u32[]{:S(2)}) copy-start(s32[8192]{0:T(1024)} %param.11) | copy-start | bytes 98308
  6.5 48.0 %all-reduce.6.cloned.1.call-start = ((), (), s32[]{:S(2)}) async-start(), calls=%async_computation.3 | async-start | bytes 525312 | tf_op jit(solution)/shard_map/psum | solution.py:21
  28.1 141.3 %all-gather.3.cloned.1.call-start = ((), (), s32[]{:S(2)}) async-start(), calls=%async_computation | async-start | bytes 20971520 | tf_op jit(solution)/shard_map/all_gather | solution.py:28
  55.1 8.2 %copy-start.1 = (f32[256,32]{1,0:T(8,128)S(1)}, f32[256,32]{1,0:T(8,128)}, u32[]{:S(2)}) copy-start(f32[256,32]{1,0:T(8,128)} %get-tuple-element.7) | copy-start | bytes 98308
  63.0 394.8 %all-gather.5.cloned.1.call-start = ((), (), s32[]{:S(2)}) async-start(), calls=%async_computation.1 | async-start | bytes 20971520 | tf_op jit(solution)/shard_map/all_gather | solution.py:31
  70.9 517.4 %all-reduce.4.cloned.1.call-start = ((), (), s32[]{:S(2)}) async-start(), calls=%async_computation.2 | async-start | bytes 8388608 | tf_op jit(solution)/shard_map/psum | solution.py:38
Sparse Core Ops, SparseCore 0:
  28.2 26.2 all-reduce.5
  63.2 106.1 all-gather.2
  171.0 286.7 all-gather.4
  482.3 106.0 all-reduce.3
where the time goes:
time: 599 us; the launch traced here: 598 us
  waiting for transfers between devices  519 us (87%)
  matrix products  58.3 us (10%)
  between operations  13.2 us (2%)
    all_gather x1, waiting for transfers between devices, on_device(): lax.all_gather(delta_reference, 'row', axis=0, tiled=True)  288 us
    psum x1, waiting for transfers between devices, on_device(): whole = lax.psum(partial_value, 'pix')  106 us
    all_gather x1, waiting for transfers between devices, on_device(): sample_rows = lax.all_gather(delta_sample, 'col', axis=0, tiled=True)  98.4 us
    psum x1, waiting for transfers between devices, on_device(): lax.psum((sums_sample, sums_reference, counts), 'pix')  26.4 us
    dot_general x1, matrix products, on_device(): lax.dot_general(sample_rows, lax.all_gather(delta_reference, 'row', axis=...  24.3 us
  transfers between devices with their start and end apart: 4, of which 4 were waited for; matrix products, arithmetic and copies ran while one was open for 1% of the time, Pallas kernels for 0%

commit v1 on v0

--- a/solution.py
+++ b/solution.py
@@ -5,6 +5,23 @@
 from jax.sharding import PartitionSpec as P
 
 QBINS = 32
+
+
+def in_order(blocks, dim):
+    shape = list(blocks.shape[1:])
+    shape[dim] *= blocks.shape[0]
+    return jnp.moveaxis(blocks, 0, dim).reshape(shape)
+
+
+def doubled(shard, axis):
+    size, index = (lax.axis_size(axis), lax.axis_index(axis))
+    tiles, distance = (shard[None], 1)
+    while distance < size:
+        other = lax.ppermute(tiles, axis, [(i, i ^ distance) for i in range(size)])
+        low = index & distance == 0
+        tiles = jnp.concatenate([jnp.where(low, tiles, other), jnp.where(low, other, tiles)])
+        distance *= 2
+    return tiles
 
 
 def on_device(sample_frames, reference_frames, gain, flat, qbin, region, live):
@@ -25,7 +42,7 @@
     spread_reference = jnp.dot(mean_reference, select, precision=lax.Precision.HIGHEST)
     delta_sample = ((corrected_sample / spread_sample - 1.0) * sample_weight).astype(jnp.bfloat16)
     delta_reference = (corrected_reference / spread_reference - 1.0).astype(jnp.bfloat16)
-    sample_rows = lax.all_gather(delta_sample, "col", axis=0, tiled=True)
+    sample_rows = in_order(doubled(delta_sample, "col"), 0)
     partial_value = lax.dot_general(
         sample_rows,
         lax.all_gather(delta_reference, "row", axis=0, tiled=True),

time: 599 us -> 491 us (0.82)
  waiting for transfers between devices: 519 us -> 383 us
  other arithmetic: 3.66 us -> 30.8 us
    all_gather x1, waiting for transfers between devices: 288 us -> 61.7 us  [on_device(): lax.all_gather(delta_reference, 'row', axis=0, tiled=True)]
    ppermute x0 -> x2, waiting for transfers between devices: none -> 189 us  [doubled(): other = lax.ppermute(tiles, axis, [(i, i ^ distance) for i in range(size)])]
    all_gather x1 -> x0, waiting for transfers between devices: 98.4 us -> none  [on_device(): sample_rows = lax.all_gather(delta_sample, 'col', axis=0, tiled=True)]
    concatenate x0 -> x2, other arithmetic: none -> 14.3 us  [doubled(): jnp.concatenate([jnp.where(low, tiles, other), jnp.where(low, other, tile...]
    select_n x0 -> x2, other arithmetic: none -> 12.7 us  [doubled(): jnp.where(low, tiles, other)]
  transfers between devices with their start and end apart: 4 -> 5, of which waited for: 4 -> 5; matrix products, arithmetic and copies ran while one was open for 1% -> 7% of each run, Pallas kernels for 0% -> 0%
where the time goes in v1:
time: 491 us
  waiting for transfers between devices  383 us (78%)
  matrix products  58.3 us (12%)
  other arithmetic  30.8 us (6%)
  between operations  13.1 us (3%)
    ppermute x2, waiting for transfers between devices, doubled(): other = lax.ppermute(tiles, axis, [(i, i ^ distance) for i in range(size)])  189 us
    psum x1, waiting for transfers between devices, on_device(): whole = lax.psum(partial_value, 'pix')  106 us
    all_gather x1, waiting for transfers between devices, on_device(): lax.all_gather(delta_reference, 'row', axis=0, tiled=True)  61.7 us
    psum x1, waiting for transfers between devices, on_device(): lax.psum((sums_sample, sums_reference, counts), 'pix')  26.4 us
    dot_general x1, matrix products, on_device(): lax.dot_general(sample_rows, lax.all_gather(delta_reference, 'row', axis=...  24.3 us
    concatenate x2, other arithmetic, doubled(): jnp.concatenate([jnp.where(low, tiles, other), jnp.where(low, other, tile...  14.3 us
    select_n x2, other arithmetic, doubled(): jnp.where(low, tiles, other)  12.7 us
  transfers between devices with their start and end apart: 5, of which 5 were waited for; matrix products, arithmetic and copies ran while one was open for 7% of the time, Pallas kernels for 0%

profile of v1, /device:TPU:0, one launch (start us, length us, event | category | flops | bytes accessed | tf_op | source)
XLA Modules:
  0.0 490.7 jit_solution(1182661555488229035)
XLA Ops:
  6.5 0.8 multiply_convert_fusion.1
  7.3 0.8 div.23
  8.1 1.6 select_reduce_fusion
  9.7 9.2 %fusion.6 = f32[256,32]{1,0:T(8,128)} fusion(bf16[256,8192]{1,0:T(8,128)(2,1)} %param.8, f32[8192]{0:T(1024)S(1)} %div.23, f32[8192]{0:T(1024)S(1)} %get-tuple-element.12, s32[8192]{0:T(1024)} %param.11), kind=kOutput, calls=%fused_computation.11 | convolution fusion | flops 810024960 | bytes 4325376 | tf_op jit(solution)/shard_map/dot_general | solution.py:36
  18.9 9.2 %fusion.7 = f32[256,32]{1,0:T(8,128)} fusion(bf16[256,8192]{1,0:T(8,128)(2,1)} %param.7, f32[8192]{0:T(1024)S(1)} %div.23, f32[8192]{0:T(1024)S(1)} %get-tuple-element.12, s32[8192]{0:T(1024)} %param.11), kind=kOutput, calls=%fused_computation.13 | convolution fusion | flops 810024960 | bytes 4325376 | tf_op jit(solution)/shard_map/dot_general | solution.py:35
  28.1 0.0 all-reduce.6.cloned.1.call-update
  28.2 0.0 all-gather.2.cloned.1.call-start
  28.2 26.4 %all-reduce.6.cloned.1.call-done = (f32[256,32]{1,0:T(8,128)}, f32[32]{0:T(128)}, f32[256,32]{1,0:T(8,128)}) async-done(((f32[256,32]{1,0:T(8,128)}, f32[32]{0:T(128)}, f32[256,32]{1,0:T(8,128)}), (f32[256,32]{1,0:T(8,128)}, f32[32]{0:T(128)}, f32[256,32]{1,0:T(8,128)})) %all-reduce.6.cloned.1.call-update) | async-done | bytes 65680 | tf_op jit(solution)/shard_map/psum | solution.py:38
  54.6 0.7 broadcast_add_fusion
  55.3 7.7 %fusion.1 = bf16[256,8192]{1,0:T(8,128)(2,1)} fusion(bf16[256,8192]{1,0:T(8,128)(2,1)} %param.8, f32[8192]{0:T(1024)S(1)} %div.23, s32[8192]{0:T(1024)S(1)} %copy-done.1, f32[256,32]{1,0:T(8,128)} %get-tuple-element.7, f32[32]{0:T(128)S(1)} %broadcast_add_fusion), kind=kOutput, calls=%fused_computation.3 | convolution fusion | flops 816070656 | bytes 8487040 | tf_op jit(solution)/shard_map/dot_general | solution.py:42
  63.0 0.2 all-reduce.4.cloned.1.call-start
  63.2 7.9 %fusion.5 = bf16[1,256,8192]{2,1,0:T(8,128)(2,1)} fusion(bf16[256,8192]{1,0:T(8,128)(2,1)} %param.7, f32[8192]{0:T(1024)S(1)} %get-tuple-element.13, f32[8192]{0:T(1024)S(1)} %div.23, s32[8192]{0:T(1024)S(1)} %copy-done.1, f32[256,32]{1,0:T(8,128)S(1)} %copy-done.2, f32[32]{0:T(128)S(1)} %broadcast_add_fusion), kind=kOutput, calls=%fused_computation.8 | convolution fusion | flops 818167808 | bytes 8519808 | tf_op jit(solution)/shard_map/dot_general | solution.py:41
  71.1 7.5 %collective-permute-done = bf16[1,256,8192]{2,1,0:T(8,128)(2,1)} collective-permute-done((bf16[1,256,8192]{2,1,0:T(8,128)(2,1)}, bf16[1,256,8192]{2,1,0:T(8,128)(2,1)}, u32[]{:S(2)}, u32[]{:S(2)}) %collective-permute-start) | collective-permute-done | bytes 4194336 | tf_op jit(solution)/shard_map/ppermute | solution.py:20
  78.6 6.4 %broadcast_select_fusion.3 = (bf16[1,256,8192]{2,1,0:T(8,128)(2,1)S(1)}, bf16[1,256,8192]{2,1,0:T(8,128)(2,1)}) fusion(bf16[1,256,8192]{2,1,0:T(8,128)(2,1)} %fusion.5, bf16[1,256,8192]{2,1,0:T(8,128)(2,1)} %collective-permute-done, pred[]{:T(512)S(6)} %eq.20), kind=kLoop, calls=%fused_computation.19 | loop fusion | flops 4194304 | bytes 16777216 | tf_op jit(solution)/shard_map/jit(_where)/select_n | solution.py:22
  85.0 7.7 %pad_maximum_fusion.1 = bf16[2,256,8192]{2,1,0:T(8,128)(2,1)} fusion(bf16[1,256,8192]{2,1,0:T(8,128)(2,1)} %get-tuple-element.11, bf16[1,256,8192]{2,1,0:T(8,128)(2,1)S(1)} %get-tuple-element.10), kind=kLoop, calls=%fused_computation.9 | loop fusion | flops 4194304 | bytes 16777216 | tf_op jit(solution)/shard_map/concatenate | solution.py:22
  92.7 1.5 collective-permute-start.1
  94.2 181.3 %collective-permute-done.1 = bf16[2,256,8192]{2,1,0:T(8,128)(2,1)} collective-permute-done((bf16[2,256,8192]{2,1,0:T(8,128)(2,1)}, bf16[2,256,8192]{2,1,0:T(8,128)(2,1)}, u32[]{:S(2)}, u32[]{:S(2)}) %collective-permute-start.1) | collective-permute-done | bytes 8388640 | tf_op jit(solution)/shard_map/ppermute | solution.py:20
  275.5 6.3 %broadcast_select_fusion.1 = (bf16[2,256,8192]{2,1,0:T(8,128)(2,1)S(1)}, bf16[2,256,8192]{2,1,0:T(8,128)(2,1)S(1)}) fusion(bf16[2,256,8192]{2,1,0:T(8,128)(2,1)} %collective-permute-done.1, pred[]{:T(512)S(6)} %eq.19, bf16[1,256,8192]{2,1,0:T(8,128)(2,1)} %get-tuple-element.11, bf16[1,256,8192]{2,1,0:T(8,128)(2,1)} %copy-done), kind=kLoop, calls=%fused_computation.15 | loop fusion | flops 12582912 | bytes 33554432 | tf_op jit(solution)/shard_map/jit(_where)/select_n | solution.py:22
  281.9 6.6 %pad_maximum_fusion = bf16[4,256,8192]{2,1,0:T(8,128)(2,1)} fusion(bf16[2,256,8192]{2,1,0:T(8,128)(2,1)S(1)} %get-tuple-element.9, bf16[2,256,8192]{2,1,0:T(8,128)(2,1)S(1)} %get-tuple-element.8), kind=kLoop, calls=%fused_computation | loop fusion | flops 8388608 | bytes 33554432 | tf_op jit(solution)/shard_map/concatenate | solution.py:22
  288.4 61.7 %all-gather.2.cloned.1.call-done = bf16[1024,8192]{1,0:T(8,128)(2,1)} async-done(((bf16[256,8192]{1,0:T(8,128)(2,1)}), bf16[1024,8192]{1,0:T(8,128)(2,1)}) %all-gather.2.cloned.1.call-update) | async-done | bytes 16777232 | tf_op jit(solution)/shard_map/all_gather | solution.py:48
  350.1 24.3 %convolution_multiply_fusion = f32[1024,1024]{0,1:T(8,128)} fusion(bf16[1024,8192]{1,0:T(8,128)(2,1)} %bitcast.7, bf16[1024,8192]{1,0:T(8,128)(2,1)} %all-gather.2.cloned.1.call-done), kind=kOutput, calls=%fused_computation.20 | convolution fusion | flops 17180917760 | bytes 37748736 | tf_op jit(solution)/shard_map/dot_general | solution.py:46
  374.5 106.2 %all-reduce.4.cloned.1.call-done = f32[1024,4,256]{0,2,1:T(8,128)} async-done(((f32[1024,4,256]{0,2,1:T(8,128)}), f32[1024,4,256]{0,2,1:T(8,128)}) %all-reduce.4.cloned.1.call-update) | async-done | bytes 4194320 | tf_op jit(solution)/shard_map/psum | solution.py:55
  480.7 1.7 constant_dynamic-slice_fusion
  482.4 1.8 copy.9
  (10 shorter events, 0.0 us)
Async XLA Ops:
  6.5 48.7 %copy-start.1 = (s32[8192]{0:T(1024)S(1)}, s32[8192]{0:T(1024)}, u32[]{:S(2)}) copy-start(s32[8192]{0:T(1024)} %param.11) | copy-start | bytes 98308
  6.5 48.0 %all-reduce.6.cloned.1.call-start = ((), (), s32[]{:S(2)}) async-start(), calls=%async_computation.2 | async-start | bytes 525312 | tf_op jit(solution)/shard_map/psum | solution.py:38
  28.2 322.0 %all-gather.2.cloned.1.call-start = ((), (), s32[]{:S(2)}) async-start(), calls=%async_computation | async-start | bytes 20971520 | tf_op jit(solution)/shard_map/all_gather | solution.py:48
  55.3 7.9 %copy-start.2 = (f32[256,32]{1,0:T(8,128)S(1)}, f32[256,32]{1,0:T(8,128)}, u32[]{:S(2)}) copy-start(f32[256,32]{1,0:T(8,128)} %get-tuple-element.5) | copy-start | bytes 98308
  63.0 417.7 %all-reduce.4.cloned.1.call-start = ((), (), s32[]{:S(2)}) async-start(), calls=%async_computation.1 | async-start | bytes 8388608 | tf_op jit(solution)/shard_map/psum | solution.py:55
  71.1 7.5 %collective-permute-start = (bf16[1,256,8192]{2,1,0:T(8,128)(2,1)}, bf16[1,256,8192]{2,1,0:T(8,128)(2,1)}, u32[]{:S(2)}, u32[]{:S(2)}) collective-permute-start(bf16[1,256,8192]{2,1,0:T(8,128)(2,1)} %fusion.5), channel_id=1, source_target_pairs={{0,2},{2,0},{4,6},{6,4},{1,3},{3,1},{5,7},{7,5},{8,10},{10,8},{12,... | collective-permute-start | bytes 12582920 | tf_op jit(solution)/shard_map/ppermute | solution.py:20
  85.0 7.7 %copy-start = (bf16[1,256,8192]{2,1,0:T(8,128)(2,1)}, bf16[1,256,8192]{2,1,0:T(8,128)(2,1)S(1)}, u32[]{:S(2)}) copy-start(bf16[1,256,8192]{2,1,0:T(8,128)(2,1)S(1)} %get-tuple-element.10) | copy-start | bytes 12582916
  92.7 182.8 %collective-permute-start.1 = (bf16[2,256,8192]{2,1,0:T(8,128)(2,1)}, bf16[2,256,8192]{2,1,0:T(8,128)(2,1)}, u32[]{:S(2)}, u32[]{:S(2)}) collective-permute-start(bf16[2,256,8192]{2,1,0:T(8,128)(2,1)} %pad_maximum_fusion.1), channel_id=1, source_target_pairs={{0,4},{2,6},{4,0},{6,2},{1,5},{3,7},{5,1},{7,3},{8,12},{10,14},{12... | collective-permute-start | bytes 25165832 | tf_op jit(solution)/shard_map/ppermute | solution.py:20
Sparse Core Ops, SparseCore 0:
  28.3 26.2 all-reduce.5
  63.1 286.9 all-gather.1
  374.6 106.0 all-reduce.3
